TPU v7x, 256 devices: a whole 4x4x8 slice. The times are simulated.
256 devices in a mesh: gx: 16 (over y, x), gy: 16 (over z, core).
Axes of the slice: x: 4, y: 4, z: 8, core: 2. Of those that a mesh axis runs over, the one named last changes fastest.
Arguments:
- energy: float32 [256, 2048, 128], P('gx', 'gy'), may hold values from 1 to 5
- coupling: float32 [256, 2048, 128], P('gx', 'gy'), may hold values from 4000 to 40000
Outputs:
- energy_next: float32 [256, 2048, 128], P('gx', 'gy')
All inputs are finite; a program needn't handle non-finite values.
Results may differ from a plain program's by a relative error of at most 0.0003.
Values sent between devices are 32-bit elements; how exact they have to be, the bound alone decides.
No kernel may reach another device: no remote copies, remote signals or barrier semaphores. Data moves between devices by JAX's collectives and lax.ppermute only.
A program may use at most 64 MiB of HBM per device.

v0:
```python
import jax
import jax.numpy as jnp
from jax import lax
from jax.sharding import PartitionSpec as P

y_weight = 0.15


def with_halo(shard, sides, width):
    for axis, dim in sides:
        size, length = (lax.axis_size(axis), shard.shape[dim])
        up = [(i, (i + 1) % size) for i in range(size - 1)]
        down = [(j, i) for i, j in up]
        last = lax.slice_in_dim(shard, length - width, length, axis=dim)
        initial = lax.slice_in_dim(shard, 0, width, axis=dim)
        before = lax.ppermute(last, axis, up)
        after = lax.ppermute(initial, axis, down)
        shard = jnp.concatenate([before, shard, after], axis=dim)
    return shard


def shifted(value, axis, steps):
    count = lax.axis_size(axis)
    initial, last = (max(0, -steps), min(count, count - steps))
    return lax.ppermute(value, axis, [(source, source + steps) for source in range(initial, last)])


def many_solve(diag_part, lower_part, upper_part, sources):

    def forward(running, row):
        prev_ratio, prev_value = running
        diag_row, lower_row, upper_row, source_row = row
        denom = diag_row - lower_row * prev_ratio
        new_ratio = upper_row / denom
        new_value = (source_row - lower_row[None] * prev_value) / denom[None]
        return ((new_ratio, new_value), (new_ratio, new_value))

    start = (jnp.zeros(diag_part.shape[1:], jnp.float32), jnp.zeros(sources.shape[1:], jnp.float32))
    _, (ratios, values) = lax.scan(forward, start, (diag_part, lower_part, upper_part, sources))

    def backward(later_value, row):
        ratio_row, value_row = row
        result = value_row - ratio_row[None] * later_value
        return (result, result)

    _, solved = lax.scan(
        backward, jnp.zeros(sources.shape[1:], jnp.float32), (ratios, values), reverse=True
    )
    return solved


def body(energy, coupling):
    padded = with_halo(energy, (("gy", 1),), 1)
    source_term = energy + y_weight * (padded[:, :-2] - 2.0 * energy + padded[:, 2:])
    height = energy.shape[0]
    inner_diag = 1.0 + coupling[: height - 1] + coupling[1:height]
    inner_lower = -coupling[: height - 1]
    inner_upper = -coupling[1:height]
    blank = jnp.zeros_like(coupling[: height - 1])
    left_source = jnp.concatenate([coupling[:1], blank[1:]], 0)
    right_source = jnp.concatenate([blank[1:], coupling[height - 1 : height]], 0)
    sources = jnp.stack([source_term[: height - 1], left_source, right_source], 1)
    solved = many_solve(inner_diag, inner_lower, inner_upper, sources)
    local_part = solved[:, 0]
    left_reply = solved[:, 1]
    right_reply = solved[:, 2]
    first_rows = jnp.stack([local_part[0], left_reply[0], right_reply[0], coupling[0]], 0)
    following = shifted(first_rows, "gx", -1)
    next_local = following[0]
    next_left = following[1]
    next_right = following[2]
    next_face = following[3]
    own_face = coupling[height - 1]
    position = lax.axis_index("gx")
    lower_coef = jnp.where(position == 0, 0.0, -own_face * left_reply[height - 2])
    middle = 1.0 + own_face + next_face - own_face * right_reply[height - 2] - next_face * next_left
    upper_coef = -next_face * next_right
    target = source_term[height - 1] + own_face * local_part[height - 2] + next_face * next_local
    bundle = jnp.stack([lower_coef, middle, upper_coef, target], 0)[None]
    gathered = lax.all_gather(bundle, "gx", axis=0, tiled=True)
    whole = many_solve(gathered[:, 1], gathered[:, 0], gathered[:, 2], gathered[:, 3][:, None])
    last_value = lax.dynamic_index_in_dim(whole[:, 0], position, 0, keepdims=False)
    previous = shifted(last_value, "gx", 1)
    interior = local_part + left_reply * previous[None] + right_reply * last_value[None]
    return jnp.concatenate([interior, last_value[None]], 0)


def solution(mesh):
    in_specs = (P("gx", "gy", None), P("gx", "gy", None))
    out_specs = P("gx", "gy", None)
    return jax.shard_map(body, mesh=mesh, in_specs=in_specs, out_specs=out_specs, check_vma=False)
```

profile of v0, /device:TPU:8, one launch (start us, length us, event | category | flops | bytes accessed | tf_op | source)
XLA Modules:
  0.0 257.6 jit_solution(15537490057633315321)
XLA Ops:
  7.4 1.7 collective-permute-start
  11.4 3.7 %select_bitcast_fusion = (f32[15,1,128,128]{3,2,0,1:T(8,128)}, f32[15,128,128]{2,1,0:T(8,128)}, f32[15,128,128]{2,1,0:T(8,128)}, f32[15,128,128]{2,1,0:T(8,128)}) fusion(f32[16,128,128]{2,1,0:T(8,128)} %param.11, pred[15]{0:T(512)(128)(4,1)} %constant.130.clone.1), kind=kLoop, calls=%fused_computation.44 | loop fusion | flops 1228800 | bytes 5898255 | tf_op jit(solution)/shard_map/stack | solution.py:62
  18.2 1.9 broadcast.28.clone
  21.2 34.4 %while.68 = (s32[]{:T(128)}, f32[128,128]{1,0:T(8,128)S(1)}, f32[3,128,128]{2,1,0:T(8,128)S(1)}, f32[15,128,128]{2,1,0:T(8,128)}, f32[15,3,128,128]{3,2,1,0:T(8,...) while((s32[]{:T(128)}, f32[128,128]{1,0:T(8,128)S(1)}, ...), condition=%wide.region_1.2_spmd.clone, body=%wide.region_0.1_spmd.clone.sunk | while | flops 262147 | bytes 1442936 | solution.py:39
  55.9 28.5 %while.69 = (s32[]{:T(128)}, f32[3,128,128]{2,1,0:T(8,128)S(1)}, f32[15,3,128,128]{3,2,1,0:T(8,128)S(1)}, f32[15,3,128,128]{3,2,1,0:T(8,128)}, f32[15,128,128]{2...) while((s32[]{:T(128)}, f32[3,128,128]{2,1,0:T(8,128)S(1)}, f32[15,3,128,128]{3,2,1,0:T(8,128)S(1)}, ...), condition=%wide.region_3.4_spmd.clone, body=%wide.region_2.3_spmd.clone.sunk | while | flops 147460 | bytes 983155 | solution.py:46
  84.5 4.6 %collective-permute-start.2 = (f32[4,128,128]{2,1,0:T(8,128)S(1)}, f32[4,128,128]{2,1,0:T(8,128)S(1)}, u32[]{:S(2)}, u32[]{:S(2)}) collective-permute-start(f32[4,128,128]{2,1,0:T(8,128)S(1)} %pad_maximum_fusion.4), channel_id=1, source_target_pairs={{16,0},{32,16},{48,32},{64,48},{80,64},{96,80},{112,96},{128,112},... | collective-permute-start | bytes 786440 | tf_op jit(solution)/shard_map/ppermute | solution.py:25
  89.1 4.8 %collective-permute-done.2 = f32[4,128,128]{2,1,0:T(8,128)S(1)} collective-permute-done((f32[4,128,128]{2,1,0:T(8,128)S(1)}, f32[4,128,128]{2,1,0:T(8,128)S(1)}, u32[]{:S(2)}, u32[]{:S(2)}) %collective-permute-start.2) | collective-permute-done | bytes 262176 | tf_op jit(solution)/shard_map/ppermute | solution.py:25
  95.6 63.9 %all-gather.3.cloned.1.call-done = f32[64,128,128]{2,1,0:T(8,128)} async-done(((f32[4,128,128]{2,1,0:T(8,128)}), f32[64,128,128]{2,1,0:T(8,128)}) %all-gather.3.cloned.1.call-update) | async-done | bytes 4194320 | tf_op jit(solution)/shard_map/all_gather | solution.py:80
  159.5 4.3 %fusion.15 = (f32[16,1,128,128]{3,2,1,0:T(8,128)}, f32[16,128,128]{2,1,0:T(8,128)}, f32[16,128,128]{2,1,0:T(8,128)}, f32[16,128,128]{2,1,0:T(8,128)}) fusion(f32[16,4,128,128]{3,2,1,0:T(8,128)} %bitcast.136), kind=kLoop, calls=%fused_computation.66 | loop fusion | bytes 8388608 | tf_op jit(solution)/shard_map/slice | solution.py:81
  164.9 49.7 %while.70 = (s32[]{:T(128)}, f32[128,128]{1,0:T(8,128)S(1)}, f32[1,128,128]{2,1,0:T(8,128)S(1)}, f32[16,128,128]{2,1,0:T(8,128)}, f32[16,1,128,128]{3,2,1,0:T(8,...) while((s32[]{:T(128)}, f32[128,128]{1,0:T(8,128)S(1)}, ...), condition=%wide.region_5.6_spmd.clone, body=%wide.region_4.5_spmd.clone.sunk | while | flops 180227 | bytes 854135 | solution.py:39
  164.9 1.6 bitcast_dynamic-update-slice_fusion.16
  168.0 1.6 bitcast_dynamic-update-slice_fusion.16
  171.1 1.6 bitcast_dynamic-update-slice_fusion.16
  174.2 1.6 bitcast_dynamic-update-slice_fusion.16
  177.3 1.6 bitcast_dynamic-update-slice_fusion.16
  180.4 1.6 bitcast_dynamic-update-slice_fusion.16
  182.0 1.6 bitcast_dynamic-update-slice_fusion.15
  183.5 1.6 bitcast_dynamic-update-slice_fusion.16
  186.6 1.6 bitcast_dynamic-update-slice_fusion.16
  189.7 1.6 bitcast_dynamic-update-slice_fusion.16
  191.3 1.6 bitcast_dynamic-update-slice_fusion.15
  192.9 1.6 bitcast_dynamic-update-slice_fusion.16
  194.4 1.6 bitcast_dynamic-update-slice_fusion.15
  196.0 1.6 bitcast_dynamic-update-slice_fusion.16
  199.1 1.6 bitcast_dynamic-update-slice_fusion.16
  202.2 1.6 bitcast_dynamic-update-slice_fusion.16
  205.3 1.6 bitcast_dynamic-update-slice_fusion.16
  208.4 1.6 bitcast_dynamic-update-slice_fusion.16
  211.5 1.6 bitcast_dynamic-update-slice_fusion.16
  215.7 24.7 %while.71 = (s32[]{:T(128)}, f32[1,128,128]{2,1,0:T(8,128)S(1)}, f32[16,1,128,128]{3,2,1,0:T(8,128)}, f32[16,1,128,128]{3,2,1,0:T(8,128)}, f32[16,128,128]{2,1,0:T(8,128)}, /*index=5*/s32[]{:T(128)}, s32[]{:T(128)}, s32[]{:T(128)}) while((s32[]{:T(128)}, f32[1,128,128]{2,1,0:T(8,128)S(1)}, f32[16,1,128,128]{3,2,1,0:T(8,128)}, ...), condition=%wide.region_7.8_spmd.clone, body=%wide.region_6.7_spmd.clone.sunk | while | flops 49156 | bytes 327791 | solution.py:46
  241.2 2.2 collective-permute-start.3
  243.4 6.1 %collective-permute-done.3 = f32[128,128]{1,0:T(8,128)S(1)} collective-permute-done((f32[128,128]{1,0:T(8,128)S(1)}, f32[128,128]{1,0:T(8,128)S(1)}, u32[]{:S(2)}, u32[]{:S(2)}) %collective-permute-start.3) | collective-permute-done | bytes 65568 | tf_op jit(solution)/shard_map/ppermute | solution.py:25
  (126 shorter events, 120.9 us)
Async XLA Ops:
  6.5 153.0 %all-gather.3.cloned.1.call-start = ((), (), s32[]{:S(2)}) async-start(), calls=%async_computation | async-start | bytes 4456448 | tf_op jit(solution)/shard_map/all_gather | solution.py:80
  7.4 8.7 %collective-permute-start = (f32[16,1,128]{2,1,0:T(1,128)S(1)}, f32[16,1,128]{2,1,0:T(1,128)S(1)}, u32[]{:S(2)}, u32[]{:S(2)}) collective-permute-start(f32[16,1,128]{2,1,0:T(1,128)S(1)} %get-tuple-element.509), channel_id=1, source_target_pairs={{0,1},{1,2},{2,3},{3,4},{4,5},{5,6},{6,7},{7,8},{8,9},{9,10},{10,1... | collective-permute-start | bytes 24584 | tf_op jit(solution)/shard_map/ppermute | solution.py:16
  9.2 7.0 %collective-permute-start.1 = (f32[16,1,128]{2,1,0:T(1,128)S(1)}, f32[16,1,128]{2,1,0:T(1,128)S(1)}, u32[]{:S(2)}, u32[]{:S(2)}) collective-permute-start(f32[16,1,128]{2,1,0:T(1,128)S(1)} %get-tuple-element.510), channel_id=1, source_target_pairs={{1,0},{2,1},{3,2},{4,3},{5,4},{6,5},{7,6},{8,7},{9,8},{10,9},{11,1... | collective-permute-start | bytes 24584 | tf_op jit(solution)/shard_map/ppermute | solution.py:17
  11.4 4.8 %copy-start.3 = (f32[16,128,128]{2,1,0:T(8,128)S(1)}, f32[16,128,128]{2,1,0:T(8,128)}, u32[]{:S(2)}) copy-start(f32[16,128,128]{2,1,0:T(8,128)} %param.10) | copy-start | bytes 3145732
  16.2 1.3 copy-start.1
  16.2 1.9 copy-start.2
  16.5 1.0 copy-start
  84.5 9.4 %collective-permute-start.2 = (f32[4,128,128]{2,1,0:T(8,128)S(1)}, f32[4,128,128]{2,1,0:T(8,128)S(1)}, u32[]{:S(2)}, u32[]{:S(2)}) collective-permute-start(f32[4,128,128]{2,1,0:T(8,128)S(1)} %pad_maximum_fusion.4), channel_id=1, source_target_pairs={{16,0},{32,16},{48,32},{64,48},{80,64},{96,80},{112,96},{128,112},... | collective-permute-start | bytes 786440 | tf_op jit(solution)/shard_map/ppermute | solution.py:25
  241.2 8.3 %collective-permute-start.3 = (f32[128,128]{1,0:T(8,128)S(1)}, f32[128,128]{1,0:T(8,128)S(1)}, u32[]{:S(2)}, u32[]{:S(2)}) collective-permute-start(f32[128,128]{1,0:T(8,128)S(1)} %get-tuple-element.507), channel_id=1, source_target_pairs={{0,16},{16,32},{32,48},{48,64},{64,80},{80,96},{96,112},{112,128},... | collective-permute-start | bytes 196616 | tf_op jit(solution)/shard_map/ppermute | solution.py:25
Sparse Core Ops, SparseCore 0:
  95.7 63.7 all-gather.2
where the time goes:
time: 262 us; the launch traced here: 258 us
  other arithmetic  131 us (50%)
  waiting for transfers between devices  74.8 us (29%)
  local copies, waits for them, and re-layouts  27.8 us (11%)
  between operations  13.6 us (5%)
  starting transfers between devices  9.76 us (4%)
    dynamic_update_slice x93, other arithmetic, many_solve(): lax.scan(forward, start, (diag_part, lower_part, upper_part, sources))  124 us
    all_gather x1, waiting for transfers between devices, body(): gathered = lax.all_gather(bundle, 'gx', axis=0, tiled=True)  63.9 us
    mul x15, local copies, waits for them, and re-layouts, backward(): result = value_row - ratio_row[None] * later_value  12.7 us
    ppermute x2, waiting for transfers between devices, shifted(): lax.ppermute(value, axis, [(source, source + steps) for source in range(i...  10.9 us
    ppermute x2, starting transfers between devices, shifted(): lax.ppermute(value, axis, [(source, source + steps) for source in range(i...  6.73 us
  transfers between devices with their start and end apart: 5, of which 3 were waited for; matrix products, arithmetic and copies ran while one was open for 2% of the time, Pallas kernels for 0%

commit v1 on v0

--- a/solution.py
+++ b/solution.py
@@ -4,6 +4,12 @@
 from jax.sharding import PartitionSpec as P
 
 y_weight = 0.15
+
+
+def _watch_leaf(q_in, dim_at):
+    q_next = list(q_in.shape[1:])
+    q_next[dim_at] *= q_in.shape[0]
+    return jnp.moveaxis(q_in, 0, dim_at).reshape(q_next)
 
 
 def with_halo(shard, sides, width):
@@ -77,7 +83,23 @@
     upper_coef = -next_face * next_right
     target = source_term[height - 1] + own_face * local_part[height - 2] + next_face * next_local
     bundle = jnp.stack([lower_coef, middle, upper_coef, target], 0)[None]
-    gathered = lax.all_gather(bundle, "gx", axis=0, tiled=True)
+    n_peers_all = lax.axis_size("gx")
+    fields = [(m, (m + 1) % n_peers_all) for m in range(n_peers_all)]
+    part_now, taken_in = ([], [])
+    shelf = [(src_i, dev_j) for dev_j, src_i in fields]
+    for q in range(n_peers_all - 1):
+        if q % 2 == 0:
+            part_now.append(
+                lax.ppermute(part_now[-1] if part_now else bundle, axis_name="gx", perm=fields)
+            )
+        else:
+            u_next = lax.ppermute(taken_in[-1] if taken_in else bundle, axis_name="gx", perm=shelf)
+            taken_in.append(u_next)
+    piece_now = jnp.stack([*part_now[::-1], bundle, *taken_in])
+    y = lax.axis_index("gx")
+    moved = y - len(part_now)
+    piece_now = piece_now[(jnp.arange(n_peers_all) - moved) % n_peers_all]
+    gathered = _watch_leaf(piece_now, 0)
     whole = many_solve(gathered[:, 1], gathered[:, 0], gathered[:, 2], gathered[:, 3][:, None])
     last_value = lax.dynamic_index_in_dim(whole[:, 0], position, 0, keepdims=False)
     previous = shifted(last_value, "gx", 1)

time: 262 us -> 296 us (1.13)
  the two profiles are of different devices: /device:TPU:8 before, /device:TPU:130 now
where the time goes in v1:
time: 296 us; the launch traced here: 291 us
  other arithmetic  132 us (45%)
  local copies, waits for them, and re-layouts  55.4 us (19%)
  waiting for transfers between devices  53.3 us (18%)
  starting transfers between devices  49.7 us (17%)
    dynamic_update_slice x93, other arithmetic, many_solve(): lax.scan(forward, start, (diag_part, lower_part, upper_part, sources))  124 us
    ppermute x8, waiting for transfers between devices, body(): lax.ppermute(part_now[-1] if part_now else bundle, axis_name='gx', perm=f...  38.1 us
    ppermute x7, starting transfers between devices, body(): lax.ppermute(taken_in[-1] if taken_in else bundle, axis_name='gx', perm=s...  28.3 us
    unnamed x50, local copies, waits for them, and re-layouts  23.2 us
    ppermute x2, waiting for transfers between devices, shifted(): lax.ppermute(value, axis, [(source, source + steps) for source in range(i...  12.9 us
    mul x15, local copies, waits for them, and re-layouts, backward(): result = value_row - ratio_row[None] * later_value  12.7 us
    ppermute x8, starting transfers between devices, body(): lax.ppermute(part_now[-1] if part_now else bundle, axis_name='gx', perm=f...  10.2 us
  transfers between devices with their start and end apart: 19, of which 14 were waited for; matrix products, arithmetic and copies ran while one was open for 9% of the time, Pallas kernels for 0%

profile of v1, /device:TPU:130, one launch (start us, length us, event | category | flops | bytes accessed | tf_op | source)
XLA Modules:
  0.0 290.6 jit_solution(3794068992273049484)
XLA Ops:
  1.0 1.9 collective-permute-start
  2.9 4.9 %collective-permute-start.1 = (f32[16,1,128]{2,1,0:T(1,128)S(1)}, f32[16,1,128]{2,1,0:T(1,128)S(1)}, u32[]{:S(2)}, u32[]{:S(2)}) collective-permute-start(f32[16,1,128]{2,1,0:T(1,128)S(1)} %get-tuple-element.501), channel_id=1, source_target_pairs={{1,0},{2,1},{3,2},{4,3},{5,4},{6,5},{7,6},{8,7},{9,8},{10,9},{11,1... | collective-permute-start | bytes 24584 | tf_op jit(solution)/shard_map/ppermute | solution.py:23
  8.7 3.7 %select_bitcast_fusion = (f32[15,1,128,128]{3,2,0,1:T(8,128)}, f32[15,128,128]{2,1,0:T(8,128)}, f32[15,128,128]{2,1,0:T(8,128)}, f32[15,128,128]{2,1,0:T(8,128)}) fusion(f32[16,128,128]{2,1,0:T(8,128)} %param.11, pred[15]{0:T(512)(128)(4,1)} %constant.146.clone.1), kind=kLoop, calls=%fused_computation.45 | loop fusion | flops 1228800 | bytes 5898255 | tf_op jit(solution)/shard_map/stack | solution.py:68
  15.5 1.9 broadcast.91.clone
  18.5 34.4 %while.68 = (s32[]{:T(128)}, f32[128,128]{1,0:T(8,128)S(1)}, f32[3,128,128]{2,1,0:T(8,128)S(1)}, f32[15,128,128]{2,1,0:T(8,128)}, f32[15,3,128,128]{3,2,1,0:T(8,...) while((s32[]{:T(128)}, f32[128,128]{1,0:T(8,128)S(1)}, ...), condition=%wide.region_1.2_spmd.clone, body=%wide.region_0.1_spmd.clone.sunk | while | flops 262147 | bytes 1442936 | solution.py:45
  53.2 28.5 %while.69 = (s32[]{:T(128)}, f32[3,128,128]{2,1,0:T(8,128)S(1)}, f32[15,3,128,128]{3,2,1,0:T(8,128)S(1)}, f32[15,3,128,128]{3,2,1,0:T(8,128)}, f32[15,128,128]{2...) while((s32[]{:T(128)}, f32[3,128,128]{2,1,0:T(8,128)S(1)}, f32[15,3,128,128]{3,2,1,0:T(8,128)S(1)}, ...), condition=%wide.region_3.4_spmd.clone, body=%wide.region_2.3_spmd.clone.sunk | while | flops 147460 | bytes 983155 | solution.py:52
  81.8 2.4 collective-permute-start.2
  84.2 5.9 %collective-permute-done.2 = f32[4,128,128]{2,1,0:T(8,128)} collective-permute-done((f32[4,128,128]{2,1,0:T(8,128)S(1)}, f32[4,128,128]{2,1,0:T(8,128)}, u32[]{:S(2)}, u32[]{:S(2)}) %collective-permute-start.2) | collective-permute-done | bytes 262176 | tf_op jit(solution)/shard_map/ppermute | solution.py:31
  92.8 4.9 %collective-permute-done.3 = f32[1,4,128,128]{3,2,1,0:T(8,128)S(1)} collective-permute-done((f32[1,4,128,128]{3,2,1,0:T(8,128)S(1)}, f32[1,4,128,128]{3,2,1,0:T(8,128)S(1)}, u32[]{:S(2)}, u32[]{:S(2)}) %collective-permute-start.3) | collective-permute-done | bytes 262176 | tf_op jit(solution)/shard_map/ppermute | solution.py:93
  98.4 2.8 collective-permute-start.4
  102.3 4.9 %collective-permute-done.4 = f32[1,4,128,128]{3,2,1,0:T(8,128)S(1)} collective-permute-done((f32[1,4,128,128]{3,2,1,0:T(8,128)S(1)}, f32[1,4,128,128]{3,2,1,0:T(8,128)S(1)}, u32[]{:S(2)}, u32[]{:S(2)}) %collective-permute-start.4) | collective-permute-done | bytes 262176 | tf_op jit(solution)/shard_map/ppermute | solution.py:93
  107.2 2.8 collective-permute-start.5
  110.7 2.0 collective-permute-start.12
  112.7 3.8 %collective-permute-done.5 = f32[1,4,128,128]{3,2,1,0:T(8,128)S(1)} collective-permute-done((f32[1,4,128,128]{3,2,1,0:T(8,128)S(1)}, f32[1,4,128,128]{3,2,1,0:T(8,128)S(1)}, u32[]{:S(2)}, u32[]{:S(2)}) %collective-permute-start.5) | collective-permute-done | bytes 262176 | tf_op jit(solution)/shard_map/ppermute | solution.py:93
  116.5 2.5 collective-permute-start.6
  119.5 2.9 collective-permute-start.13
  122.4 4.9 %collective-permute-done.6 = f32[1,4,128,128]{3,2,1,0:T(8,128)S(1)} collective-permute-done((f32[1,4,128,128]{3,2,1,0:T(8,128)S(1)}, f32[1,4,128,128]{3,2,1,0:T(8,128)S(1)}, u32[]{:S(2)}, u32[]{:S(2)}) %collective-permute-start.6) | collective-permute-done | bytes 262176 | tf_op jit(solution)/shard_map/ppermute | solution.py:93
  128.6 5.1 %collective-permute-start.14 = (f32[1,4,128,128]{3,2,1,0:T(8,128)S(1)}, f32[1,4,128,128]{3,2,1,0:T(8,128)S(1)}, u32[]{:S(2)}, u32[]{:S(2)}) collective-permute-start(f32[1,4,128,128]{3,2,1,0:T(8,128)S(1)} %collective-permute-done.13), channel_id=1, source_target_pairs={{16,0},{32,16},{48,32},{64,48},{80,64},{96,80},{112,96},{128,112},... | collective-permute-start | bytes 786440 | tf_op jit(solution)/shard_map/ppermute | solution.py:96
  133.7 5.7 %collective-permute-done.7 = f32[1,4,128,128]{3,2,1,0:T(8,128)S(1)} collective-permute-done((f32[1,4,128,128]{3,2,1,0:T(8,128)S(1)}, f32[1,4,128,128]{3,2,1,0:T(8,128)S(1)}, u32[]{:S(2)}, u32[]{:S(2)}) %collective-permute-start.7) | collective-permute-done | bytes 262176 | tf_op jit(solution)/shard_map/ppermute | solution.py:93
  140.2 6.0 %collective-permute-start.15 = (f32[1,4,128,128]{3,2,1,0:T(8,128)S(1)}, f32[1,4,128,128]{3,2,1,0:T(8,128)}, u32[]{:S(2)}, u32[]{:S(2)}) collective-permute-start(f32[1,4,128,128]{3,2,1,0:T(8,128)S(1)} %collective-permute-done.14), channel_id=1, source_target_pairs={{16,0},{32,16},{48,32},{64,48},{80,64},{96,80},{112,96},{128,112},... | collective-permute-start | bytes 786440 | tf_op jit(solution)/shard_map/ppermute | solution.py:96
  146.2 5.5 %collective-permute-done.8 = f32[1,4,128,128]{3,2,1,0:T(8,128)S(1)} collective-permute-done((f32[1,4,128,128]{3,2,1,0:T(8,128)S(1)}, f32[1,4,128,128]{3,2,1,0:T(8,128)S(1)}, u32[]{:S(2)}, u32[]{:S(2)}) %collective-permute-start.8) | collective-permute-done | bytes 262176 | tf_op jit(solution)/shard_map/ppermute | solution.py:93
  152.3 5.6 %collective-permute-start.16 = (f32[1,4,128,128]{3,2,1,0:T(8,128)}, f32[1,4,128,128]{3,2,1,0:T(8,128)}, u32[]{:S(2)}, u32[]{:S(2)}) collective-permute-start(f32[1,4,128,128]{3,2,1,0:T(8,128)} %collective-permute-done.15), channel_id=1, source_target_pairs={{16,0},{32,16},{48,32},{64,48},{80,64},{96,80},{112,96},{128,112},... | collective-permute-start | bytes 786440 | tf_op jit(solution)/shard_map/ppermute | solution.py:96
  157.9 4.9 %collective-permute-done.9 = f32[1,4,128,128]{3,2,1,0:T(8,128)} collective-permute-done((f32[1,4,128,128]{3,2,1,0:T(8,128)S(1)}, f32[1,4,128,128]{3,2,1,0:T(8,128)}, u32[]{:S(2)}, u32[]{:S(2)}) %collective-permute-start.9) | collective-permute-done | bytes 262176 | tf_op jit(solution)/shard_map/ppermute | solution.py:93
  163.3 5.8 %collective-permute-start.17 = (f32[1,4,128,128]{3,2,1,0:T(8,128)}, f32[1,4,128,128]{3,2,1,0:T(8,128)S(1)}, u32[]{:S(2)}, u32[]{:S(2)}) collective-permute-start(f32[1,4,128,128]{3,2,1,0:T(8,128)} %collective-permute-done.16), channel_id=1, source_target_pairs={{16,0},{32,16},{48,32},{64,48},{80,64},{96,80},{112,96},{128,112},... | collective-permute-start | bytes 786440 | tf_op jit(solution)/shard_map/ppermute | solution.py:96
  169.1 3.4 %collective-permute-done.10 = f32[1,4,128,128]{3,2,1,0:T(8,128)} collective-permute-done((f32[1,4,128,128]{3,2,1,0:T(8,128)}, f32[1,4,128,128]{3,2,1,0:T(8,128)}, u32[]{:S(2)}, u32[]{:S(2)}) %collective-permute-start.10) | collective-permute-done | bytes 262176 | tf_op jit(solution)/shard_map/ppermute | solution.py:93
  189.5 1.7 bitcast_dynamic-update-slice_fusion.8
  193.6 5.0 %gather_fusion = f32[16,4,128,128]{3,2,1,0:T(8,128)} fusion(f32[16,4,128,128]{3,2,1,0:T(8,128)} %bitcast.28, s32[1024]{0:T(1024)S(1)} %pad_clamp_fusion), kind=kCustom, calls=%fused_computation | custom fusion | bytes 8388672 | tf_op jit(solution)/shard_map/gather | solution.py:101
  198.6 4.3 %fusion.18 = (f32[16,1,128,128]{3,2,1,0:T(8,128)}, f32[16,128,128]{2,1,0:T(8,128)}, f32[16,128,128]{2,1,0:T(8,128)}, f32[16,128,128]{2,1,0:T(8,128)}) fusion(f32[16,4,128,128]{3,2,1,0:T(8,128)} %gather_fusion), kind=kLoop, calls=%fused_computation.91 | loop fusion | bytes 8388608 | tf_op jit(solution)/shard_map/slice | solution.py:103
  204.1 49.8 %while.70 = (s32[]{:T(128)}, f32[128,128]{1,0:T(8,128)S(1)}, f32[1,128,128]{2,1,0:T(8,128)S(1)}, f32[16,128,128]{2,1,0:T(8,128)}, f32[16,1,128,128]{3,2,1,0:T(8,...) while((s32[]{:T(128)}, f32[128,128]{1,0:T(8,128)S(1)}, ...), condition=%wide.region_5.6_spmd.clone, body=%wide.region_4.5_spmd.clone.sunk | while | flops 180227 | bytes 854135 | solution.py:45
  254.9 24.7 %while.71 = (s32[]{:T(128)}, f32[1,128,128]{2,1,0:T(8,128)S(1)}, f32[16,1,128,128]{3,2,1,0:T(8,128)}, f32[16,1,128,128]{3,2,1,0:T(8,128)}, f32[16,128,128]{2,1,0:T(8,128)}, /*index=5*/s32[]{:T(128)}, s32[]{:T(128)}, s32[]{:T(128)}) while((s32[]{:T(128)}, f32[1,128,128]{2,1,0:T(8,128)S(1)}, f32[16,1,128,128]{3,2,1,0:T(8,128)}, ...), condition=%wide.region_7.8_spmd.clone, body=%wide.region_6.7_spmd.clone.sunk | while | flops 49156 | bytes 327791 | solution.py:52
  280.5 1.9 collective-permute-start.18
  282.4 6.9 %collective-permute-done.18 = f32[128,128]{1,0:T(8,128)S(1)} collective-permute-done((f32[128,128]{1,0:T(8,128)S(1)}, f32[128,128]{1,0:T(8,128)S(1)}, u32[]{:S(2)}, u32[]{:S(2)}) %collective-permute-start.18) | collective-permute-done | bytes 65568 | tf_op jit(solution)/shard_map/ppermute | solution.py:31
  (200 shorter events, 175.9 us)
Async XLA Ops:
  0.0 13.4 %copy-start.3 = (f32[16,128,128]{2,1,0:T(8,128)S(1)}, f32[16,128,128]{2,1,0:T(8,128)}, u32[]{:S(2)}) copy-start(f32[16,128,128]{2,1,0:T(8,128)} %param.10) | copy-start | bytes 3145732
  1.0 12.4 %collective-permute-start = (f32[16,1,128]{2,1,0:T(1,128)S(1)}, f32[16,1,128]{2,1,0:T(1,128)S(1)}, u32[]{:S(2)}, u32[]{:S(2)}) collective-permute-start(f32[16,1,128]{2,1,0:T(1,128)S(1)} %get-tuple-element.500), channel_id=1, source_target_pairs={{0,1},{1,2},{2,3},{3,4},{4,5},{5,6},{6,7},{7,8},{8,9},{9,10},{10,1... | collective-permute-start | bytes 24584 | tf_op jit(solution)/shard_map/ppermute | solution.py:22
  2.9 10.5 %collective-permute-start.1 = (f32[16,1,128]{2,1,0:T(1,128)S(1)}, f32[16,1,128]{2,1,0:T(1,128)S(1)}, u32[]{:S(2)}, u32[]{:S(2)}) collective-permute-start(f32[16,1,128]{2,1,0:T(1,128)S(1)} %get-tuple-element.501), channel_id=1, source_target_pairs={{1,0},{2,1},{3,2},{4,3},{5,4},{6,5},{7,6},{8,7},{9,8},{10,9},{11,1... | collective-permute-start | bytes 24584 | tf_op jit(solution)/shard_map/ppermute | solution.py:23
  13.4 1.9 copy-start.2
  81.8 8.4 %collective-permute-start.2 = (f32[4,128,128]{2,1,0:T(8,128)S(1)}, f32[4,128,128]{2,1,0:T(8,128)}, u32[]{:S(2)}, u32[]{:S(2)}) collective-permute-start(f32[4,128,128]{2,1,0:T(8,128)S(1)} %pad_maximum_fusion.4), channel_id=1, source_target_pairs={{16,0},{32,16},{48,32},{64,48},{80,64},{96,80},{112,96},{128,112},... | collective-permute-start | bytes 786440 | tf_op jit(solution)/shard_map/ppermute | solution.py:31
  91.3 6.5 %collective-permute-start.3 = (f32[1,4,128,128]{3,2,1,0:T(8,128)S(1)}, f32[1,4,128,128]{3,2,1,0:T(8,128)S(1)}, u32[]{:S(2)}, u32[]{:S(2)}) collective-permute-start(f32[1,4,128,128]{3,2,1,0:T(8,128)S(1)} %fusion.10), channel_id=1, source_target_pairs={{0,16},{16,32},{32,48},{48,64},{64,80},{80,96},{96,112},{112,128},... | collective-permute-start | bytes 786440 | tf_op jit(solution)/shard_map/ppermute | solution.py:93
  98.4 8.8 %collective-permute-start.4 = (f32[1,4,128,128]{3,2,1,0:T(8,128)S(1)}, f32[1,4,128,128]{3,2,1,0:T(8,128)S(1)}, u32[]{:S(2)}, u32[]{:S(2)}) collective-permute-start(f32[1,4,128,128]{3,2,1,0:T(8,128)S(1)} %collective-permute-done.3), channel_id=1, source_target_pairs={{0,16},{16,32},{32,48},{48,64},{64,80},{80,96},{96,112},{112,128},... | collective-permute-start | bytes 786440 | tf_op jit(solution)/shard_map/ppermute | solution.py:93
  101.2 8.7 %collective-permute-start.11 = (f32[1,4,128,128]{3,2,1,0:T(8,128)S(1)}, f32[1,4,128,128]{3,2,1,0:T(8,128)S(1)}, u32[]{:S(2)}, u32[]{:S(2)}) collective-permute-start(f32[1,4,128,128]{3,2,1,0:T(8,128)S(1)} %fusion.10), channel_id=1, source_target_pairs={{16,0},{32,16},{48,32},{64,48},{80,64},{96,80},{112,96},{128,112},... | collective-permute-start | bytes 786440 | tf_op jit(solution)/shard_map/ppermute | solution.py:96
  107.2 12.3 %copy-start.7 = (f32[1,4,128,128]{3,2,1,0:T(8,128)}, f32[1,4,128,128]{3,2,1,0:T(8,128)S(1)}, u32[]{:S(2)}) copy-start(f32[1,4,128,128]{3,2,1,0:T(8,128)S(1)} %collective-permute-done.4) | copy-start | bytes 786436
  107.2 9.3 %collective-permute-start.5 = (f32[1,4,128,128]{3,2,1,0:T(8,128)S(1)}, f32[1,4,128,128]{3,2,1,0:T(8,128)S(1)}, u32[]{:S(2)}, u32[]{:S(2)}) collective-permute-start(f32[1,4,128,128]{3,2,1,0:T(8,128)S(1)} %collective-permute-done.4), channel_id=1, source_target_pairs={{0,16},{16,32},{32,48},{48,64},{64,80},{80,96},{96,112},{112,128},... | collective-permute-start | bytes 786440 | tf_op jit(solution)/shard_map/ppermute | solution.py:93
  110.7 8.8 %collective-permute-start.12 = (f32[1,4,128,128]{3,2,1,0:T(8,128)S(1)}, f32[1,4,128,128]{3,2,1,0:T(8,128)S(1)}, u32[]{:S(2)}, u32[]{:S(2)}) collective-permute-start(f32[1,4,128,128]{3,2,1,0:T(8,128)S(1)} %collective-permute-done.11), channel_id=1, source_target_pairs={{16,0},{32,16},{48,32},{64,48},{80,64},{96,80},{112,96},{128,112},... | collective-permute-start | bytes 786440 | tf_op jit(solution)/shard_map/ppermute | solution.py:96
  116.5 12.2 %copy-start.10 = (f32[1,4,128,128]{3,2,1,0:T(8,128)}, f32[1,4,128,128]{3,2,1,0:T(8,128)S(1)}, u32[]{:S(2)}) copy-start(f32[1,4,128,128]{3,2,1,0:T(8,128)S(1)} %collective-permute-done.5) | copy-start | bytes 786436
  116.5 10.8 %collective-permute-start.6 = (f32[1,4,128,128]{3,2,1,0:T(8,128)S(1)}, f32[1,4,128,128]{3,2,1,0:T(8,128)S(1)}, u32[]{:S(2)}, u32[]{:S(2)}) collective-permute-start(f32[1,4,128,128]{3,2,1,0:T(8,128)S(1)} %collective-permute-done.5), channel_id=1, source_target_pairs={{0,16},{16,32},{32,48},{48,64},{64,80},{80,96},{96,112},{112,128},... | collective-permute-start | bytes 786440 | tf_op jit(solution)/shard_map/ppermute | solution.py:93
  119.5 2.9 copy-start.8
  119.5 9.1 %collective-permute-start.13 = (f32[1,4,128,128]{3,2,1,0:T(8,128)S(1)}, f32[1,4,128,128]{3,2,1,0:T(8,128)S(1)}, u32[]{:S(2)}, u32[]{:S(2)}) collective-permute-start(f32[1,4,128,128]{3,2,1,0:T(8,128)S(1)} %collective-permute-done.12), channel_id=1, source_target_pairs={{16,0},{32,16},{48,32},{64,48},{80,64},{96,80},{112,96},{128,112},... | collective-permute-start | bytes 786440 | tf_op jit(solution)/shard_map/ppermute | solution.py:96
  127.3 25.0 %copy-start.15 = (f32[1,4,128,128]{3,2,1,0:T(8,128)}, f32[1,4,128,128]{3,2,1,0:T(8,128)S(1)}, u32[]{:S(2)}) copy-start(f32[1,4,128,128]{3,2,1,0:T(8,128)S(1)} %collective-permute-done.6) | copy-start | bytes 786436
  127.3 12.2 %collective-permute-start.7 = (f32[1,4,128,128]{3,2,1,0:T(8,128)S(1)}, f32[1,4,128,128]{3,2,1,0:T(8,128)S(1)}, u32[]{:S(2)}, u32[]{:S(2)}) collective-permute-start(f32[1,4,128,128]{3,2,1,0:T(8,128)S(1)} %collective-permute-done.6), channel_id=1, source_target_pairs={{0,16},{16,32},{32,48},{48,64},{64,80},{80,96},{96,112},{112,128},... | collective-permute-start | bytes 786440 | tf_op jit(solution)/shard_map/ppermute | solution.py:93
  128.6 5.1 %copy-start.11 = (f32[1,4,128,128]{3,2,1,0:T(8,128)}, f32[1,4,128,128]{3,2,1,0:T(8,128)S(1)}, u32[]{:S(2)}) copy-start(f32[1,4,128,128]{3,2,1,0:T(8,128)S(1)} %collective-permute-done.13) | copy-start | bytes 786436
  128.6 10.8 %collective-permute-start.14 = (f32[1,4,128,128]{3,2,1,0:T(8,128)S(1)}, f32[1,4,128,128]{3,2,1,0:T(8,128)S(1)}, u32[]{:S(2)}, u32[]{:S(2)}) collective-permute-start(f32[1,4,128,128]{3,2,1,0:T(8,128)S(1)} %collective-permute-done.13), channel_id=1, source_target_pairs={{16,0},{32,16},{48,32},{64,48},{80,64},{96,80},{112,96},{128,112},... | collective-permute-start | bytes 786440 | tf_op jit(solution)/shard_map/ppermute | solution.py:96
  139.4 18.4 %copy-start.16 = (f32[1,4,128,128]{3,2,1,0:T(8,128)}, f32[1,4,128,128]{3,2,1,0:T(8,128)S(1)}, u32[]{:S(2)}) copy-start(f32[1,4,128,128]{3,2,1,0:T(8,128)S(1)} %collective-permute-done.7) | copy-start | bytes 786436
  139.5 12.2 %collective-permute-start.8 = (f32[1,4,128,128]{3,2,1,0:T(8,128)S(1)}, f32[1,4,128,128]{3,2,1,0:T(8,128)S(1)}, u32[]{:S(2)}, u32[]{:S(2)}) collective-permute-start(f32[1,4,128,128]{3,2,1,0:T(8,128)S(1)} %collective-permute-done.7), channel_id=1, source_target_pairs={{0,16},{16,32},{32,48},{48,64},{64,80},{80,96},{96,112},{112,128},... | collective-permute-start | bytes 786440 | tf_op jit(solution)/shard_map/ppermute | solution.py:93
  140.2 12.1 %collective-permute-start.15 = (f32[1,4,128,128]{3,2,1,0:T(8,128)S(1)}, f32[1,4,128,128]{3,2,1,0:T(8,128)}, u32[]{:S(2)}, u32[]{:S(2)}) collective-permute-start(f32[1,4,128,128]{3,2,1,0:T(8,128)S(1)} %collective-permute-done.14), channel_id=1, source_target_pairs={{16,0},{32,16},{48,32},{64,48},{80,64},{96,80},{112,96},{128,112},... | collective-permute-start | bytes 786440 | tf_op jit(solution)/shard_map/ppermute | solution.py:96
  151.7 11.1 %copy-start.17 = (f32[1,4,128,128]{3,2,1,0:T(8,128)}, f32[1,4,128,128]{3,2,1,0:T(8,128)S(1)}, u32[]{:S(2)}) copy-start(f32[1,4,128,128]{3,2,1,0:T(8,128)S(1)} %collective-permute-done.8) | copy-start | bytes 786436
  151.7 11.1 %collective-permute-start.9 = (f32[1,4,128,128]{3,2,1,0:T(8,128)S(1)}, f32[1,4,128,128]{3,2,1,0:T(8,128)}, u32[]{:S(2)}, u32[]{:S(2)}) collective-permute-start(f32[1,4,128,128]{3,2,1,0:T(8,128)S(1)} %collective-permute-done.8), channel_id=1, source_target_pairs={{0,16},{16,32},{32,48},{48,64},{64,80},{80,96},{96,112},{112,128},... | collective-permute-start | bytes 786440 | tf_op jit(solution)/shard_map/ppermute | solution.py:93
  152.3 11.1 %collective-permute-start.16 = (f32[1,4,128,128]{3,2,1,0:T(8,128)}, f32[1,4,128,128]{3,2,1,0:T(8,128)}, u32[]{:S(2)}, u32[]{:S(2)}) collective-permute-start(f32[1,4,128,128]{3,2,1,0:T(8,128)} %collective-permute-done.15), channel_id=1, source_target_pairs={{16,0},{32,16},{48,32},{64,48},{80,64},{96,80},{112,96},{128,112},... | collective-permute-start | bytes 786440 | tf_op jit(solution)/shard_map/ppermute | solution.py:96
  162.8 9.7 %collective-permute-start.10 = (f32[1,4,128,128]{3,2,1,0:T(8,128)}, f32[1,4,128,128]{3,2,1,0:T(8,128)}, u32[]{:S(2)}, u32[]{:S(2)}) collective-permute-start(f32[1,4,128,128]{3,2,1,0:T(8,128)} %collective-permute-done.9), channel_id=1, source_target_pairs={{0,16},{16,32},{32,48},{48,64},{64,80},{80,96},{96,112},{112,128},... | collective-permute-start | bytes 786440 | tf_op jit(solution)/shard_map/ppermute | solution.py:93
  162.8 23.8 %copy-start.6 = (f32[1,4,128,128]{3,2,1,0:T(8,128)S(1)}, f32[1,4,128,128]{3,2,1,0:T(8,128)}, u32[]{:S(2)}) copy-start(f32[1,4,128,128]{3,2,1,0:T(8,128)} %copy-done.5) | copy-start | bytes 786436
  162.9 24.5 %copy-start.9 = (f32[1,4,128,128]{3,2,1,0:T(8,128)S(1)}, f32[1,4,128,128]{3,2,1,0:T(8,128)}, u32[]{:S(2)}) copy-start(f32[1,4,128,128]{3,2,1,0:T(8,128)} %copy-done.8) | copy-start | bytes 786436
  162.9 25.2 %copy-start.12 = (f32[1,4,128,128]{3,2,1,0:T(8,128)S(1)}, f32[1,4,128,128]{3,2,1,0:T(8,128)}, u32[]{:S(2)}) copy-start(f32[1,4,128,128]{3,2,1,0:T(8,128)} %copy-done.11) | copy-start | bytes 786436
  162.9 25.9 %copy-start.14 = (f32[1,4,128,128]{3,2,1,0:T(8,128)S(1)}, f32[1,4,128,128]{3,2,1,0:T(8,128)}, u32[]{:S(2)}) copy-start(f32[1,4,128,128]{3,2,1,0:T(8,128)} %copy-done.13) | copy-start | bytes 786436
  163.3 29.6 %collective-permute-start.17 = (f32[1,4,128,128]{3,2,1,0:T(8,128)}, f32[1,4,128,128]{3,2,1,0:T(8,128)S(1)}, u32[]{:S(2)}, u32[]{:S(2)}) collective-permute-start(f32[1,4,128,128]{3,2,1,0:T(8,128)} %collective-permute-done.16), channel_id=1, source_target_pairs={{16,0},{32,16},{48,32},{64,48},{80,64},{96,80},{112,96},{128,112},... | collective-permute-start | bytes 786440 | tf_op jit(solution)/shard_map/ppermute | solution.py:96
  280.5 8.9 %collective-permute-start.18 = (f32[128,128]{1,0:T(8,128)S(1)}, f32[128,128]{1,0:T(8,128)S(1)}, u32[]{:S(2)}, u32[]{:S(2)}) collective-permute-start(f32[128,128]{1,0:T(8,128)S(1)} %get-tuple-element.498), channel_id=1, source_target_pairs={{0,16},{16,32},{32,48},{48,64},{64,80},{80,96},{96,112},{112,128},... | collective-permute-start | bytes 196616 | tf_op jit(solution)/shard_map/ppermute | solution.py:31
  (5 other events, 4.5 us)
